TPU v7x, 32 devices: a whole 2x2x4 slice. The times are simulated.
32 devices in a mesh: ctx: 8 (over z, y), tp: 4 (over x, core).
Axes of the slice: x: 2, y: 2, z: 4, core: 2. Of those that a mesh axis runs over, the one named last changes fastest.
Arguments:
- queries: bfloat16 [2048, 16, 128], P('ctx', 'tp'), may hold values from -12 to 12
- keys: bfloat16 [2048, 8, 128], P('ctx', 'tp'), may hold values from -6 to 6
- values: bfloat16 [2048, 8, 128], P('ctx', 'tp'), may hold values from -6 to 6
- residual: bfloat16 [2048, 3072], P('ctx', 'tp'), may hold values from -6 to 6
- out_weight: bfloat16 [16, 128, 3072], P(None, None, 'tp'), may hold values from -1 to 1
- post_gain: bfloat16 [3072], P('tp'), may hold values from 0.099609375 to 1.8984375
Outputs:
- mixed: bfloat16 [2048, 3072], P('ctx', 'tp')
All inputs are finite; a program needn't handle non-finite values.
Results may differ from a plain program's by a relative error of at most 0.015.
Values may be sent and summed in bfloat16 or wider, within the bound.
No kernel may reach another device: no remote copies, remote signals or barrier semaphores. Data moves between devices by JAX's collectives and lax.ppermute only.
A program may use at most 64 MiB of HBM per device.

v0:
```python
import jax
import jax.numpy as jnp
from jax import lax
from jax.sharding import PartitionSpec as P

WINDOW_TOKENS = 4096
D = 3072
softcap_value = 50.0
query_scale = 1.0 / 12.0
rope_base = 10000.0


def passed_along(value, axis, steps):
    count = lax.axis_size(axis)
    first, last = (max(0, -steps), min(count, count - steps))
    return lax.ppermute(value, axis, [(source, source + steps) for source in range(first, last)])


def rotate(values_in, positions):
    half_width = values_in.shape[-1] // 2
    steps_half = jnp.arange(half_width, dtype=jnp.float32)
    inverse = rope_base ** (-2.0 * steps_half / values_in.shape[-1])
    angles = positions.astype(jnp.float32)[..., None] * inverse
    cosine = jnp.cos(angles)
    sine_part = jnp.sin(angles)
    first_half = values_in[..., :half_width]
    second_half = values_in[..., half_width:]
    return jnp.concatenate(
        [
            first_half * cosine - second_half * sine_part,
            second_half * cosine + first_half * sine_part,
        ],
        axis=-1,
    )


def attend_block(state, key_block, value_block, source, rotary_queries, device_index):
    numerators, denominators = state
    rows = key_block.shape[0]
    scores = (
        jnp.einsum("sgrh,kgh->grsk", rotary_queries, key_block, preferred_element_type=jnp.float32)
        * query_scale
    )
    capped = softcap_value * jnp.tanh(scores / softcap_value)
    offsets = jnp.arange(rows, dtype=jnp.int32)
    query_pos = device_index * rows + offsets
    key_pos = source * rows + offsets
    distance = query_pos[:, None] - key_pos[None, :]
    allowed = (distance >= 0) & (distance < WINDOW_TOKENS) & (key_pos[None, :] >= 0)
    weights = jnp.where(allowed[None, None], jnp.exp(capped), 0.0)
    denominators = denominators + jnp.sum(weights, axis=-1)
    numerators = numerators + jnp.einsum(
        "grsk,kgh->grsh",
        weights.astype(jnp.bfloat16),
        value_block,
        preferred_element_type=jnp.float32,
    )
    return (numerators, denominators)


def local(queries, keys, values, residual, out_weight, post_gain):
    rows = queries.shape[0]
    q_heads = queries.shape[1]
    head_size = queries.shape[2]
    kv_heads = keys.shape[1]
    heads_per_group = q_heads // kv_heads
    cycle_size = lax.axis_size("ctx")
    device_index = lax.axis_index("ctx")
    positions = (device_index * rows + jnp.arange(rows, dtype=jnp.int32))[:, None]
    rotary_queries = rotate(queries.astype(jnp.float32), positions).astype(jnp.bfloat16)
    rotary_queries = rotary_queries.reshape(rows, kv_heads, heads_per_group, head_size)
    rotary_keys = rotate(keys.astype(jnp.float32), positions).astype(jnp.bfloat16)
    reach = min(WINDOW_TOKENS // rows, cycle_size - 1)
    state = (
        jnp.zeros((kv_heads, heads_per_group, rows, head_size), jnp.float32),
        jnp.zeros((kv_heads, heads_per_group, rows), jnp.float32),
    )
    state = attend_block(state, rotary_keys, values, device_index, rotary_queries, device_index)

    def advance(step_index, carried):
        running, key_block, value_block = carried
        key_block, value_block = passed_along((key_block, value_block), "ctx", 1)
        running = attend_block(
            running,
            key_block,
            value_block,
            device_index - step_index - 1,
            rotary_queries,
            device_index,
        )
        return (running, key_block, value_block)

    state, unused_keys, unused_values = lax.fori_loop(
        0, reach, advance, (state, rotary_keys, values)
    )
    numerators, denominators = state
    attended = (numerators / denominators[..., None]).astype(jnp.bfloat16)
    attended = jnp.transpose(attended, (2, 0, 1, 3)).reshape(rows, q_heads, head_size)
    local_cols = out_weight.shape[2]
    piece = lax.all_gather(attended, "tp", axis=1, tiled=True)
    heads_in = piece.shape[1]
    weight_rows = out_weight.reshape(heads_in * head_size, local_cols)
    projected = jnp.dot(
        piece.reshape(rows, heads_in * head_size), weight_rows, preferred_element_type=jnp.float32
    )
    square_sums = lax.psum(jnp.sum(projected * projected, axis=1), "tp")
    normed = projected * lax.rsqrt(square_sums / D + 1e-06)[:, None] * post_gain.astype(jnp.float32)
    mixed = residual.astype(jnp.float32) + normed
    return mixed.astype(jnp.bfloat16)


def solution(mesh):
    in_specs = (
        P("ctx", "tp", None),
        P("ctx", "tp", None),
        P("ctx", "tp", None),
        P("ctx", "tp"),
        P(None, None, "tp"),
        P("tp"),
    )
    out_specs = P("ctx", "tp")
    return jax.shard_map(local, mesh=mesh, in_specs=in_specs, out_specs=out_specs, check_vma=False)
```

profile of v0, /device:TPU:0, one launch (start us, length us, event | category | flops | bytes accessed | tf_op | source)
XLA Modules:
  0.0 137.2 jit_solution(11933492602181658960)
XLA Ops:
  16.1 85.1 %while.21 = (s32[]{:T(128)}, f32[2,2,256,128]{3,2,1,0:T(8,128)}, f32[2,2,256]{2,1,0:T(2,128)S(1)}, bf16[256,2,128]{2,0,1:T(8,128)(2,1)}, bf16[256,2,128]{2,0,1:T...) while((s32[]{:T(128)}, f32[2,2,256,128]{3,2,1,0:T(8,128)}, ...), condition=%wide.region_3.4_spmd, body=%wide.region_1.3_spmd.sunk | while | flops 135988224 | bytes 8540965 | solution.py:93
  16.1 4.9 %collective-permute-start = (bf16[256,2,128]{2,0,1:T(8,128)(2,1)}, bf16[256,2,128]{2,0,1:T(8,128)(2,1)S(1)}, u32[]{:S(2)}, u32[]{:S(2)}) collective-permute-start(bf16[256,2,128]{2,0,1:T(8,128)(2,1)} %get-tuple-element.308), channel_id=1, source_target_pairs={{0,4},{4,8},{8,12},{12,16},{16,20},{20,24},{24,28},{1,5},{5,9},{9,... | collective-permute-start | bytes 393224 | tf_op jit(solution)/shard_map/while/body/eval_jaxpr/ppermute | solution.py:16
  21.0 3.4 %collective-permute-start.1 = (bf16[256,2,128]{2,0,1:T(8,128)(2,1)S(1)}, bf16[256,2,128]{2,0,1:T(8,128)(2,1)S(1)}, u32[]{:S(2)}, u32[]{:S(2)}) collective-permute-start(bf16[256,2,128]{2,0,1:T(8,128)(2,1)S(1)} %get-tuple-element.309), channel_id=1, source_target_pairs={{0,4},{4,8},{8,12},{12,16},{16,20},{20,24},{24,28},{1,5},{5,9},{9,... | collective-permute-start | bytes 393224 | tf_op jit(solution)/shard_map/while/body/eval_jaxpr/ppermute | solution.py:16
  24.7 1.4 %fusion.40 = (f32[2,2,256]{2,1,0:T(2,128)S(1)}, bf16[2,2,256,256]{2,3,1,0:T(8,128)(2,1)S(1)}) fusion(bf16[256,2,2,128]{3,0,2,1:T(8,128)(2,1)} %get-tuple-element.323, bf16[256,2,128]{2,0,1:T(8,128)(2,1)S(1)} %collective-permute-done, pred[256,256]{0,1:T(8,128)(4,1)S(1)} %fusion.39), kind=kOutput, calls=%fused_computation.49.clone.1 | convolution fusion | flops 68418560 | bytes 987136 | tf_op jit(solution)/shard_map/while/body/eval_jaxpr/sgrh,kgh->grsk/dot_general | solution.py:41
  28.2 4.3 %collective-permute-start = (bf16[256,2,128]{2,0,1:T(8,128)(2,1)}, bf16[256,2,128]{2,0,1:T(8,128)(2,1)S(1)}, u32[]{:S(2)}, u32[]{:S(2)}) collective-permute-start(bf16[256,2,128]{2,0,1:T(8,128)(2,1)} %get-tuple-element.308), channel_id=1, source_target_pairs={{0,4},{4,8},{8,12},{12,16},{16,20},{20,24},{24,28},{1,5},{5,9},{9,... | collective-permute-start | bytes 393224 | tf_op jit(solution)/shard_map/while/body/eval_jaxpr/ppermute | solution.py:16
  32.5 4.3 %collective-permute-start.1 = (bf16[256,2,128]{2,0,1:T(8,128)(2,1)S(1)}, bf16[256,2,128]{2,0,1:T(8,128)(2,1)S(1)}, u32[]{:S(2)}, u32[]{:S(2)}) collective-permute-start(bf16[256,2,128]{2,0,1:T(8,128)(2,1)S(1)} %get-tuple-element.309), channel_id=1, source_target_pairs={{0,4},{4,8},{8,12},{12,16},{16,20},{20,24},{24,28},{1,5},{5,9},{9,... | collective-permute-start | bytes 393224 | tf_op jit(solution)/shard_map/while/body/eval_jaxpr/ppermute | solution.py:16
  40.6 4.3 %collective-permute-start = (bf16[256,2,128]{2,0,1:T(8,128)(2,1)}, bf16[256,2,128]{2,0,1:T(8,128)(2,1)S(1)}, u32[]{:S(2)}, u32[]{:S(2)}) collective-permute-start(bf16[256,2,128]{2,0,1:T(8,128)(2,1)} %get-tuple-element.308), channel_id=1, source_target_pairs={{0,4},{4,8},{8,12},{12,16},{16,20},{20,24},{24,28},{1,5},{5,9},{9,... | collective-permute-start | bytes 393224 | tf_op jit(solution)/shard_map/while/body/eval_jaxpr/ppermute | solution.py:16
  45.0 4.1 %collective-permute-start.1 = (bf16[256,2,128]{2,0,1:T(8,128)(2,1)S(1)}, bf16[256,2,128]{2,0,1:T(8,128)(2,1)S(1)}, u32[]{:S(2)}, u32[]{:S(2)}) collective-permute-start(bf16[256,2,128]{2,0,1:T(8,128)(2,1)S(1)} %get-tuple-element.309), channel_id=1, source_target_pairs={{0,4},{4,8},{8,12},{12,16},{16,20},{20,24},{24,28},{1,5},{5,9},{9,... | collective-permute-start | bytes 393224 | tf_op jit(solution)/shard_map/while/body/eval_jaxpr/ppermute | solution.py:16
  52.8 4.4 %collective-permute-start = (bf16[256,2,128]{2,0,1:T(8,128)(2,1)}, bf16[256,2,128]{2,0,1:T(8,128)(2,1)S(1)}, u32[]{:S(2)}, u32[]{:S(2)}) collective-permute-start(bf16[256,2,128]{2,0,1:T(8,128)(2,1)} %get-tuple-element.308), channel_id=1, source_target_pairs={{0,4},{4,8},{8,12},{12,16},{16,20},{20,24},{24,28},{1,5},{5,9},{9,... | collective-permute-start | bytes 393224 | tf_op jit(solution)/shard_map/while/body/eval_jaxpr/ppermute | solution.py:16
  57.2 3.7 %collective-permute-start.1 = (bf16[256,2,128]{2,0,1:T(8,128)(2,1)S(1)}, bf16[256,2,128]{2,0,1:T(8,128)(2,1)S(1)}, u32[]{:S(2)}, u32[]{:S(2)}) collective-permute-start(bf16[256,2,128]{2,0,1:T(8,128)(2,1)S(1)} %get-tuple-element.309), channel_id=1, source_target_pairs={{0,4},{4,8},{8,12},{12,16},{16,20},{20,24},{24,28},{1,5},{5,9},{9,... | collective-permute-start | bytes 393224 | tf_op jit(solution)/shard_map/while/body/eval_jaxpr/ppermute | solution.py:16
  61.1 1.4 %fusion.40 = (f32[2,2,256]{2,1,0:T(2,128)S(1)}, bf16[2,2,256,256]{2,3,1,0:T(8,128)(2,1)S(1)}) fusion(bf16[256,2,2,128]{3,0,2,1:T(8,128)(2,1)} %get-tuple-element.323, bf16[256,2,128]{2,0,1:T(8,128)(2,1)S(1)} %collective-permute-done, pred[256,256]{0,1:T(8,128)(4,1)S(1)} %fusion.39), kind=kOutput, calls=%fused_computation.49.clone.1 | convolution fusion | flops 68418560 | bytes 987136 | tf_op jit(solution)/shard_map/while/body/eval_jaxpr/sgrh,kgh->grsk/dot_general | solution.py:41
  64.6 4.3 %collective-permute-start = (bf16[256,2,128]{2,0,1:T(8,128)(2,1)}, bf16[256,2,128]{2,0,1:T(8,128)(2,1)S(1)}, u32[]{:S(2)}, u32[]{:S(2)}) collective-permute-start(bf16[256,2,128]{2,0,1:T(8,128)(2,1)} %get-tuple-element.308), channel_id=1, source_target_pairs={{0,4},{4,8},{8,12},{12,16},{16,20},{20,24},{24,28},{1,5},{5,9},{9,... | collective-permute-start | bytes 393224 | tf_op jit(solution)/shard_map/while/body/eval_jaxpr/ppermute | solution.py:16
  69.0 4.1 %collective-permute-start.1 = (bf16[256,2,128]{2,0,1:T(8,128)(2,1)S(1)}, bf16[256,2,128]{2,0,1:T(8,128)(2,1)S(1)}, u32[]{:S(2)}, u32[]{:S(2)}) collective-permute-start(bf16[256,2,128]{2,0,1:T(8,128)(2,1)S(1)} %get-tuple-element.309), channel_id=1, source_target_pairs={{0,4},{4,8},{8,12},{12,16},{16,20},{20,24},{24,28},{1,5},{5,9},{9,... | collective-permute-start | bytes 393224 | tf_op jit(solution)/shard_map/while/body/eval_jaxpr/ppermute | solution.py:16
  76.8 4.3 %collective-permute-start = (bf16[256,2,128]{2,0,1:T(8,128)(2,1)}, bf16[256,2,128]{2,0,1:T(8,128)(2,1)S(1)}, u32[]{:S(2)}, u32[]{:S(2)}) collective-permute-start(bf16[256,2,128]{2,0,1:T(8,128)(2,1)} %get-tuple-element.308), channel_id=1, source_target_pairs={{0,4},{4,8},{8,12},{12,16},{16,20},{20,24},{24,28},{1,5},{5,9},{9,... | collective-permute-start | bytes 393224 | tf_op jit(solution)/shard_map/while/body/eval_jaxpr/ppermute | solution.py:16
  81.1 3.7 %collective-permute-start.1 = (bf16[256,2,128]{2,0,1:T(8,128)(2,1)S(1)}, bf16[256,2,128]{2,0,1:T(8,128)(2,1)S(1)}, u32[]{:S(2)}, u32[]{:S(2)}) collective-permute-start(bf16[256,2,128]{2,0,1:T(8,128)(2,1)S(1)} %get-tuple-element.309), channel_id=1, source_target_pairs={{0,4},{4,8},{8,12},{12,16},{16,20},{20,24},{24,28},{1,5},{5,9},{9,... | collective-permute-start | bytes 393224 | tf_op jit(solution)/shard_map/while/body/eval_jaxpr/ppermute | solution.py:16
  85.0 1.4 %fusion.40 = (f32[2,2,256]{2,1,0:T(2,128)S(1)}, bf16[2,2,256,256]{2,3,1,0:T(8,128)(2,1)S(1)}) fusion(bf16[256,2,2,128]{3,0,2,1:T(8,128)(2,1)} %get-tuple-element.323, bf16[256,2,128]{2,0,1:T(8,128)(2,1)S(1)} %collective-permute-done, pred[256,256]{0,1:T(8,128)(4,1)S(1)} %fusion.39), kind=kOutput, calls=%fused_computation.49.clone.1 | convolution fusion | flops 68418560 | bytes 987136 | tf_op jit(solution)/shard_map/while/body/eval_jaxpr/sgrh,kgh->grsk/dot_general | solution.py:41
  88.6 4.3 %collective-permute-start = (bf16[256,2,128]{2,0,1:T(8,128)(2,1)}, bf16[256,2,128]{2,0,1:T(8,128)(2,1)S(1)}, u32[]{:S(2)}, u32[]{:S(2)}) collective-permute-start(bf16[256,2,128]{2,0,1:T(8,128)(2,1)} %get-tuple-element.308), channel_id=1, source_target_pairs={{0,4},{4,8},{8,12},{12,16},{16,20},{20,24},{24,28},{1,5},{5,9},{9,... | collective-permute-start | bytes 393224 | tf_op jit(solution)/shard_map/while/body/eval_jaxpr/ppermute | solution.py:16
  92.9 4.6 %collective-permute-start.1 = (bf16[256,2,128]{2,0,1:T(8,128)(2,1)S(1)}, bf16[256,2,128]{2,0,1:T(8,128)(2,1)S(1)}, u32[]{:S(2)}, u32[]{:S(2)}) collective-permute-start(bf16[256,2,128]{2,0,1:T(8,128)(2,1)S(1)} %get-tuple-element.309), channel_id=1, source_target_pairs={{0,4},{4,8},{8,12},{12,16},{16,20},{20,24},{24,28},{1,5},{5,9},{9,... | collective-permute-start | bytes 393224 | tf_op jit(solution)/shard_map/while/body/eval_jaxpr/ppermute | solution.py:16
  97.7 1.4 %fusion.40 = (f32[2,2,256]{2,1,0:T(2,128)S(1)}, bf16[2,2,256,256]{2,3,1,0:T(8,128)(2,1)S(1)}) fusion(bf16[256,2,2,128]{3,0,2,1:T(8,128)(2,1)} %get-tuple-element.323, bf16[256,2,128]{2,0,1:T(8,128)(2,1)S(1)} %collective-permute-done, pred[256,256]{0,1:T(8,128)(4,1)S(1)} %fusion.39), kind=kOutput, calls=%fused_computation.49.clone.1 | convolution fusion | flops 68418560 | bytes 987136 | tf_op jit(solution)/shard_map/while/body/eval_jaxpr/sgrh,kgh->grsk/dot_general | solution.py:41
  101.2 2.0 %divide_convert_fusion = bf16[2,2,256,128]{3,2,1,0:T(8,128)(2,1)} fusion(f32[2,2,256,128]{3,2,1,0:T(8,128)} %get-tuple-element.189, f32[2,2,256]{2,1,0:T(2,128)S(1)} %get-tuple-element.190), kind=kLoop, calls=%fused_computation.26 | loop fusion | flops 262144 | bytes 790528 | tf_op jit(solution)/shard_map/convert_element_type | solution.py:97
  103.9 15.4 %all-gather.2.cloned.1.call-done = bf16[256,16,128]{2,0,1:T(8,128)(2,1)} async-done(((bf16[256,4,128]{2,0,1:T(8,128)(2,1)}), bf16[256,16,128]{2,0,1:T(8,128)(2,1)}) %all-gather.2.cloned.1.call-update) | async-done | bytes 1048592 | tf_op jit(solution)/shard_map/all_gather | solution.py:100
  119.3 3.1 %multiply_reduce_fusion = (f32[256]{0:T(256)S(1)}, f32[256,768]{1,0:T(8,128)}) fusion(bf16[256,16,128]{2,0,1:T(8,128)(2,1)} %all-gather.2.cloned.1.call-done, bf16[16,128,768]{2,1,0:T(8,128)(2,1)S(1)} %copy-done), kind=kOutput, calls=%fused_computation.25 | convolution fusion | flops 805699328 | bytes 4981760 | tf_op jit(solution)/shard_map/dot_general | solution.py:103
  122.4 5.9 %psum.7 = f32[256]{0:T(256)S(1)} all-reduce(f32[256]{0:T(256)S(1)} %get-tuple-element.233), channel_id=1, replica_groups=mesh['ctx'=8,'tp'=4] {'tp'}, use_global_device_ids=true, to_apply=%region_5.6 | all-reduce | flops 256 | bytes 2048 | tf_op jit(solution)/shard_map/psum | solution.py:106
  128.3 2.1 %add_convert_fusion = bf16[256,768]{1,0:T(8,128)(2,1)} fusion(f32[256,768]{1,0:T(8,128)} %get-tuple-element.234, bf16[256,768]{1,0:T(8,128)(2,1)S(1)} %copy-done.4, f32[768]{0:T(1024)S(1)} %convert_element_type.50, f32[256]{0:T(256)S(1)} %add_rsqrt_fusion), kind=kLoop, calls=%fused_computation.24 | loop fusion | flops 983040 | bytes 1576960 | tf_op jit(solution)/shard_map/convert_element_type | solution.py:109
  (133 shorter events, 30.1 us)
Async XLA Ops:
  6.5 112.8 %copy-start = (bf16[16,128,768]{2,1,0:T(8,128)(2,1)S(1)}, bf16[16,128,768]{2,1,0:T(8,128)(2,1)}, u32[]{:S(2)}) copy-start(bf16[16,128,768]{2,1,0:T(8,128)(2,1)} %param.12) | copy-start | bytes 9437188
  6.5 4.8 %copy-start.3 = (bf16[256,2,128]{2,1,0:T(2,128)(2,1)S(1)}, bf16[256,2,128]{2,1,0:T(2,128)(2,1)}, u32[]{:S(2)}) copy-start(bf16[256,2,128]{2,1,0:T(2,128)(2,1)} %param.10) | copy-start | bytes 393220
  6.5 112.8 %all-gather.2.cloned.1.call-start = ((), (), s32[]{:S(2)}) async-start(), calls=%async_computation | async-start | bytes 1310720 | tf_op jit(solution)/shard_map/all_gather | solution.py:100
  13.1 3.0 %copy-start.6 = (bf16[256,2,128]{2,0,1:T(8,128)(2,1)}, bf16[256,2,128]{2,0,1:T(8,128)(2,1)S(1)}, u32[]{:S(2)}) copy-start(bf16[256,2,128]{2,0,1:T(8,128)(2,1)S(1)} %pad_maximum_fusion.1) | copy-start | bytes 393220
  16.1 8.5 %collective-permute-start = (bf16[256,2,128]{2,0,1:T(8,128)(2,1)}, bf16[256,2,128]{2,0,1:T(8,128)(2,1)S(1)}, u32[]{:S(2)}, u32[]{:S(2)}) collective-permute-start(bf16[256,2,128]{2,0,1:T(8,128)(2,1)} %get-tuple-element.308), channel_id=1, source_target_pairs={{0,4},{4,8},{8,12},{12,16},{16,20},{20,24},{24,28},{1,5},{5,9},{9,... | collective-permute-start | bytes 393224 | tf_op jit(solution)/shard_map/while/body/eval_jaxpr/ppermute | solution.py:16
  21.0 5.9 %collective-permute-start.1 = (bf16[256,2,128]{2,0,1:T(8,128)(2,1)S(1)}, bf16[256,2,128]{2,0,1:T(8,128)(2,1)S(1)}, u32[]{:S(2)}, u32[]{:S(2)}) collective-permute-start(bf16[256,2,128]{2,0,1:T(8,128)(2,1)S(1)} %get-tuple-element.309), channel_id=1, source_target_pairs={{0,4},{4,8},{8,12},{12,16},{16,20},{20,24},{24,28},{1,5},{5,9},{9,... | collective-permute-start | bytes 393224 | tf_op jit(solution)/shard_map/while/body/eval_jaxpr/ppermute | solution.py:16
  24.5 2.5 %copy-start.1 = (f32[2,2,256,128]{3,2,1,0:T(8,128)S(1)}, f32[2,2,256,128]{3,2,1,0:T(8,128)}, u32[]{:S(2)}) copy-start(f32[2,2,256,128]{3,2,1,0:T(8,128)} %get-tuple-element.306) | copy-start | bytes 1572868 | tf_op jit(solution)/shard_map/while
  28.2 8.9 %collective-permute-start = (bf16[256,2,128]{2,0,1:T(8,128)(2,1)}, bf16[256,2,128]{2,0,1:T(8,128)(2,1)S(1)}, u32[]{:S(2)}, u32[]{:S(2)}) collective-permute-start(bf16[256,2,128]{2,0,1:T(8,128)(2,1)} %get-tuple-element.308), channel_id=1, source_target_pairs={{0,4},{4,8},{8,12},{12,16},{16,20},{20,24},{24,28},{1,5},{5,9},{9,... | collective-permute-start | bytes 393224 | tf_op jit(solution)/shard_map/while/body/eval_jaxpr/ppermute | solution.py:16
  32.5 6.8 %collective-permute-start.1 = (bf16[256,2,128]{2,0,1:T(8,128)(2,1)S(1)}, bf16[256,2,128]{2,0,1:T(8,128)(2,1)S(1)}, u32[]{:S(2)}, u32[]{:S(2)}) collective-permute-start(bf16[256,2,128]{2,0,1:T(8,128)(2,1)S(1)} %get-tuple-element.309), channel_id=1, source_target_pairs={{0,4},{4,8},{8,12},{12,16},{16,20},{20,24},{24,28},{1,5},{5,9},{9,... | collective-permute-start | bytes 393224 | tf_op jit(solution)/shard_map/while/body/eval_jaxpr/ppermute | solution.py:16
  36.9 2.5 %copy-start.1 = (f32[2,2,256,128]{3,2,1,0:T(8,128)S(1)}, f32[2,2,256,128]{3,2,1,0:T(8,128)}, u32[]{:S(2)}) copy-start(f32[2,2,256,128]{3,2,1,0:T(8,128)} %get-tuple-element.306) | copy-start | bytes 1572868 | tf_op jit(solution)/shard_map/while
  40.6 8.7 %collective-permute-start = (bf16[256,2,128]{2,0,1:T(8,128)(2,1)}, bf16[256,2,128]{2,0,1:T(8,128)(2,1)S(1)}, u32[]{:S(2)}, u32[]{:S(2)}) collective-permute-start(bf16[256,2,128]{2,0,1:T(8,128)(2,1)} %get-tuple-element.308), channel_id=1, source_target_pairs={{0,4},{4,8},{8,12},{12,16},{16,20},{20,24},{24,28},{1,5},{5,9},{9,... | collective-permute-start | bytes 393224 | tf_op jit(solution)/shard_map/while/body/eval_jaxpr/ppermute | solution.py:16
  45.0 6.6 %collective-permute-start.1 = (bf16[256,2,128]{2,0,1:T(8,128)(2,1)S(1)}, bf16[256,2,128]{2,0,1:T(8,128)(2,1)S(1)}, u32[]{:S(2)}, u32[]{:S(2)}) collective-permute-start(bf16[256,2,128]{2,0,1:T(8,128)(2,1)S(1)} %get-tuple-element.309), channel_id=1, source_target_pairs={{0,4},{4,8},{8,12},{12,16},{16,20},{20,24},{24,28},{1,5},{5,9},{9,... | collective-permute-start | bytes 393224 | tf_op jit(solution)/shard_map/while/body/eval_jaxpr/ppermute | solution.py:16
  49.1 2.5 %copy-start.1 = (f32[2,2,256,128]{3,2,1,0:T(8,128)S(1)}, f32[2,2,256,128]{3,2,1,0:T(8,128)}, u32[]{:S(2)}) copy-start(f32[2,2,256,128]{3,2,1,0:T(8,128)} %get-tuple-element.306) | copy-start | bytes 1572868 | tf_op jit(solution)/shard_map/while
  52.8 8.2 %collective-permute-start = (bf16[256,2,128]{2,0,1:T(8,128)(2,1)}, bf16[256,2,128]{2,0,1:T(8,128)(2,1)S(1)}, u32[]{:S(2)}, u32[]{:S(2)}) collective-permute-start(bf16[256,2,128]{2,0,1:T(8,128)(2,1)} %get-tuple-element.308), channel_id=1, source_target_pairs={{0,4},{4,8},{8,12},{12,16},{16,20},{20,24},{24,28},{1,5},{5,9},{9,... | collective-permute-start | bytes 393224 | tf_op jit(solution)/shard_map/while/body/eval_jaxpr/ppermute | solution.py:16
  57.2 6.2 %collective-permute-start.1 = (bf16[256,2,128]{2,0,1:T(8,128)(2,1)S(1)}, bf16[256,2,128]{2,0,1:T(8,128)(2,1)S(1)}, u32[]{:S(2)}, u32[]{:S(2)}) collective-permute-start(bf16[256,2,128]{2,0,1:T(8,128)(2,1)S(1)} %get-tuple-element.309), channel_id=1, source_target_pairs={{0,4},{4,8},{8,12},{12,16},{16,20},{20,24},{24,28},{1,5},{5,9},{9,... | collective-permute-start | bytes 393224 | tf_op jit(solution)/shard_map/while/body/eval_jaxpr/ppermute | solution.py:16
  60.9 2.5 %copy-start.1 = (f32[2,2,256,128]{3,2,1,0:T(8,128)S(1)}, f32[2,2,256,128]{3,2,1,0:T(8,128)}, u32[]{:S(2)}) copy-start(f32[2,2,256,128]{3,2,1,0:T(8,128)} %get-tuple-element.306) | copy-start | bytes 1572868 | tf_op jit(solution)/shard_map/while
  64.6 8.6 %collective-permute-start = (bf16[256,2,128]{2,0,1:T(8,128)(2,1)}, bf16[256,2,128]{2,0,1:T(8,128)(2,1)S(1)}, u32[]{:S(2)}, u32[]{:S(2)}) collective-permute-start(bf16[256,2,128]{2,0,1:T(8,128)(2,1)} %get-tuple-element.308), channel_id=1, source_target_pairs={{0,4},{4,8},{8,12},{12,16},{16,20},{20,24},{24,28},{1,5},{5,9},{9,... | collective-permute-start | bytes 393224 | tf_op jit(solution)/shard_map/while/body/eval_jaxpr/ppermute | solution.py:16
  69.0 6.6 %collective-permute-start.1 = (bf16[256,2,128]{2,0,1:T(8,128)(2,1)S(1)}, bf16[256,2,128]{2,0,1:T(8,128)(2,1)S(1)}, u32[]{:S(2)}, u32[]{:S(2)}) collective-permute-start(bf16[256,2,128]{2,0,1:T(8,128)(2,1)S(1)} %get-tuple-element.309), channel_id=1, source_target_pairs={{0,4},{4,8},{8,12},{12,16},{16,20},{20,24},{24,28},{1,5},{5,9},{9,... | collective-permute-start | bytes 393224 | tf_op jit(solution)/shard_map/while/body/eval_jaxpr/ppermute | solution.py:16
  73.1 2.5 %copy-start.1 = (f32[2,2,256,128]{3,2,1,0:T(8,128)S(1)}, f32[2,2,256,128]{3,2,1,0:T(8,128)}, u32[]{:S(2)}) copy-start(f32[2,2,256,128]{3,2,1,0:T(8,128)} %get-tuple-element.306) | copy-start | bytes 1572868 | tf_op jit(solution)/shard_map/while
  76.8 8.2 %collective-permute-start = (bf16[256,2,128]{2,0,1:T(8,128)(2,1)}, bf16[256,2,128]{2,0,1:T(8,128)(2,1)S(1)}, u32[]{:S(2)}, u32[]{:S(2)}) collective-permute-start(bf16[256,2,128]{2,0,1:T(8,128)(2,1)} %get-tuple-element.308), channel_id=1, source_target_pairs={{0,4},{4,8},{8,12},{12,16},{16,20},{20,24},{24,28},{1,5},{5,9},{9,... | collective-permute-start | bytes 393224 | tf_op jit(solution)/shard_map/while/body/eval_jaxpr/ppermute | solution.py:16
  81.1 6.2 %collective-permute-start.1 = (bf16[256,2,128]{2,0,1:T(8,128)(2,1)S(1)}, bf16[256,2,128]{2,0,1:T(8,128)(2,1)S(1)}, u32[]{:S(2)}, u32[]{:S(2)}) collective-permute-start(bf16[256,2,128]{2,0,1:T(8,128)(2,1)S(1)} %get-tuple-element.309), channel_id=1, source_target_pairs={{0,4},{4,8},{8,12},{12,16},{16,20},{20,24},{24,28},{1,5},{5,9},{9,... | collective-permute-start | bytes 393224 | tf_op jit(solution)/shard_map/while/body/eval_jaxpr/ppermute | solution.py:16
  88.6 9.1 %collective-permute-start = (bf16[256,2,128]{2,0,1:T(8,128)(2,1)}, bf16[256,2,128]{2,0,1:T(8,128)(2,1)S(1)}, u32[]{:S(2)}, u32[]{:S(2)}) collective-permute-start(bf16[256,2,128]{2,0,1:T(8,128)(2,1)} %get-tuple-element.308), channel_id=1, source_target_pairs={{0,4},{4,8},{8,12},{12,16},{16,20},{20,24},{24,28},{1,5},{5,9},{9,... | collective-permute-start | bytes 393224 | tf_op jit(solution)/shard_map/while/body/eval_jaxpr/ppermute | solution.py:16
  92.9 7.1 %collective-permute-start.1 = (bf16[256,2,128]{2,0,1:T(8,128)(2,1)S(1)}, bf16[256,2,128]{2,0,1:T(8,128)(2,1)S(1)}, u32[]{:S(2)}, u32[]{:S(2)}) collective-permute-start(bf16[256,2,128]{2,0,1:T(8,128)(2,1)S(1)} %get-tuple-element.309), channel_id=1, source_target_pairs={{0,4},{4,8},{8,12},{12,16},{16,20},{20,24},{24,28},{1,5},{5,9},{9,... | collective-permute-start | bytes 393224 | tf_op jit(solution)/shard_map/while/body/eval_jaxpr/ppermute | solution.py:16
  101.2 27.1 %copy-start.4 = (bf16[256,768]{1,0:T(8,128)(2,1)S(1)}, bf16[256,768]{1,0:T(8,128)(2,1)}, u32[]{:S(2)}) copy-start(bf16[256,768]{1,0:T(8,128)(2,1)} %param.11) | copy-start | bytes 1179652
  (11 other events, 14.2 us)
Sparse Core Ops, SparseCore 0:
  103.4 15.8 all-gather.1
where the time goes:
time: 138 us; the launch traced here: 137 us
  starting transfers between devices  58.8 us (43%)
  matrix products  17.8 us (13%)
  waiting for transfers between devices  16.7 us (12%)
  between operations  13.5 us (10%)
  other arithmetic  12.3 us (9%)
  local copies, waits for them, and re-layouts  11.6 us (8%)
  blocking collectives  5.85 us (4%)
    ppermute x14, starting transfers between devices, passed_along(): lax.ppermute(value, axis, [(source, source + steps) for source in range(f...  58.8 us
    all_gather x1, waiting for transfers between devices, local(): piece = lax.all_gather(attended, 'tp', axis=1, tiled=True)  15.4 us
    dot_general x8, matrix products, attend_block(): jnp.einsum('sgrh,kgh->grsk', rotary_queries, key_block, preferred_element...  10.6 us
    while x42, local copies, waits for them, and re-layouts  10.1 us
    psum x1, blocking collectives, local(): square_sums = lax.psum(jnp.sum(projected * projected, axis=1), 'tp')  5.85 us
    dot_general x8, matrix products, attend_block(): jnp.einsum('grsk,kgh->grsh', weights.astype(jnp.bfloat16), value_block, p...  4.09 us
    dot_general x1, matrix products, local(): jnp.dot(piece.reshape(rows, heads_in * head_size), weight_rows, preferred...  3.14 us
  transfers between devices with their start and end apart: 15, of which 8 were waited for; matrix products, arithmetic and copies ran while one was open for 12% of the time, Pallas kernels for 0%

commit v1 on v0

--- a/solution.py
+++ b/solution.py
@@ -97,7 +97,23 @@
     attended = (numerators / denominators[..., None]).astype(jnp.bfloat16)
     attended = jnp.transpose(attended, (2, 0, 1, 3)).reshape(rows, q_heads, head_size)
     local_cols = out_weight.shape[2]
-    piece = lax.all_gather(attended, "tp", axis=1, tiled=True)
+    size, index, span = (lax.axis_size("tp"), lax.axis_index("tp"), attended.shape[1])
+    right = [(i, (i + 1) % size) for i in range(size)]
+    left = [(i, (i - 1) % size) for i in range(size)]
+    piece = jnp.zeros((*attended.shape[:1], size * span, *attended.shape[1 + 1 :]), attended.dtype)
+    piece = lax.dynamic_update_slice_in_dim(piece, attended, index * span, axis=1)
+    from_left = from_right = attended
+    halfway = size // 2
+    for step in range(1, halfway + 1):
+        from_left = lax.ppermute(from_left, "tp", right)
+        piece = lax.dynamic_update_slice_in_dim(
+            piece, from_left, (index - step) % size * span, axis=1
+        )
+        if step < size - halfway:
+            from_right = lax.ppermute(from_right, "tp", left)
+            piece = lax.dynamic_update_slice_in_dim(
+                piece, from_right, (index + step) % size * span, axis=1
+            )
     heads_in = piece.shape[1]
     weight_rows = out_weight.reshape(heads_in * head_size, local_cols)
     projected = jnp.dot(

time: 138 us -> 129 us (0.935)
  between operations: 13.5 us -> 0.11 us
  local copies, waits for them, and re-layouts: 11.6 us -> 18.7 us
  waiting for transfers between devices: 16.7 us -> 13 us
  blocking collectives: 5.85 us -> 8.17 us
  other arithmetic: 12.3 us -> 10.7 us
    all_gather x1 -> x0, waiting for transfers between devices: 15.4 us -> none  [local(): piece = lax.all_gather(attended, 'tp', axis=1, tiled=True)]
    ppermute x14, waiting for transfers between devices: 1.3 us -> 7.89 us  [passed_along(): lax.ppermute(value, axis, [(source, source + steps) for source in range(f...]
    dynamic_update_slice x0 -> x4, local copies, waits for them, and re-layouts: none -> 5.78 us  [the longest x2 3.39 us: local(): lax.dynamic_update_slice_in_dim(piece, from_left, (index - step) % size *...]
    ppermute x0 -> x3, waiting for transfers between devices: none -> 5.14 us  [the longest x2 5.14 us: local(): from_left = lax.ppermute(from_left, 'tp', right)]
    psum x1, blocking collectives: 5.85 us -> 8.17 us  [local(): square_sums = lax.psum(jnp.sum(projected * projected, axis=1), 'tp')]
    ppermute x0 -> x3, starting transfers between devices: none -> 1.93 us  [the longest x1 1.73 us: local(): from_right = lax.ppermute(from_right, 'tp', left)]
    ppermute x14, starting transfers between devices: 58.8 us -> 57 us  [passed_along(): lax.ppermute(value, axis, [(source, source + steps) for source in range(f...]
  transfers between devices with their start and end apart: 15 -> 17, of which waited for: 8 -> 8; matrix products, arithmetic and copies ran while one was open for 12% -> 13% of each run, Pallas kernels for 0% -> 0%
where the time goes in v1:
time: 129 us; the launch traced here: 128 us
  starting transfers between devices  59 us (46%)
  local copies, waits for them, and re-layouts  18.7 us (14%)
  matrix products  17.8 us (14%)
  waiting for transfers between devices  13 us (10%)
  other arithmetic  10.7 us (8%)
  blocking collectives  8.17 us (6%)
    ppermute x14, starting transfers between devices, passed_along(): lax.ppermute(value, axis, [(source, source + steps) for source in range(f...  57 us
    dot_general x8, matrix products, attend_block(): jnp.einsum('sgrh,kgh->grsk', rotary_queries, key_block, preferred_element...  10.6 us
    while x42, local copies, waits for them, and re-layouts  10.2 us
    psum x1, blocking collectives, local(): square_sums = lax.psum(jnp.sum(projected * projected, axis=1), 'tp')  8.17 us
    ppermute x14, waiting for transfers between devices, passed_along(): lax.ppermute(value, axis, [(source, source + steps) for source in range(f...  7.89 us
    ppermute x2, waiting for transfers between devices, local(): from_left = lax.ppermute(from_left, 'tp', right)  5.14 us
    dot_general x8, matrix products, attend_block(): jnp.einsum('grsk,kgh->grsh', weights.astype(jnp.bfloat16), value_block, p...  4.09 us
    dynamic_update_slice x2, local copies, waits for them, and re-layouts, local(): lax.dynamic_update_slice_in_dim(piece, from_left, (index - step) % size *...  3.39 us
  transfers between devices with their start and end apart: 17, of which 8 were waited for; matrix products, arithmetic and copies ran while one was open for 13% of the time, Pallas kernels for 0%

profile of v1, /device:TPU:0, one launch (start us, length us, event | category | flops | bytes accessed | tf_op | source)
XLA Modules:
  0.0 128.2 jit_solution(11443161821394218355)
XLA Ops:
  8.8 90.0 %while.21 = (s32[]{:T(128)}, f32[2,2,256,128]{3,2,1,0:T(8,128)}, f32[2,2,256]{2,1,0:T(2,128)S(1)}, bf16[256,2,128]{2,0,1:T(8,128)(2,1)S(1)}, bf16[256,2,128]{2,0...) while((s32[]{:T(128)}, f32[2,2,256,128]{3,2,1,0:T(8,128)}, ...), condition=%wide.region_3.4_spmd, body=%wide.region_1.3_spmd.sunk | while | flops 135988224 | bytes 8540965 | solution.py:93
  8.8 4.9 %collective-permute-start = (bf16[256,2,128]{2,0,1:T(8,128)(2,1)S(1)}, bf16[256,2,128]{2,0,1:T(8,128)(2,1)S(1)}, u32[]{:S(2)}, u32[]{:S(2)}) collective-permute-start(bf16[256,2,128]{2,0,1:T(8,128)(2,1)S(1)} %get-tuple-element.300), channel_id=1, source_target_pairs={{0,4},{4,8},{8,12},{12,16},{16,20},{20,24},{24,28},{1,5},{5,9},{9,... | collective-permute-start | bytes 393224 | tf_op jit(solution)/shard_map/while/body/eval_jaxpr/ppermute | solution.py:16
  13.6 3.4 %collective-permute-start.1 = (bf16[256,2,128]{2,0,1:T(8,128)(2,1)}, bf16[256,2,128]{2,0,1:T(8,128)(2,1)S(1)}, u32[]{:S(2)}, u32[]{:S(2)}) collective-permute-start(bf16[256,2,128]{2,0,1:T(8,128)(2,1)} %get-tuple-element.301), channel_id=1, source_target_pairs={{0,4},{4,8},{8,12},{12,16},{16,20},{20,24},{24,28},{1,5},{5,9},{9,... | collective-permute-start | bytes 393224 | tf_op jit(solution)/shard_map/while/body/eval_jaxpr/ppermute | solution.py:16
  21.8 4.2 %collective-permute-start = (bf16[256,2,128]{2,0,1:T(8,128)(2,1)S(1)}, bf16[256,2,128]{2,0,1:T(8,128)(2,1)S(1)}, u32[]{:S(2)}, u32[]{:S(2)}) collective-permute-start(bf16[256,2,128]{2,0,1:T(8,128)(2,1)S(1)} %get-tuple-element.300), channel_id=1, source_target_pairs={{0,4},{4,8},{8,12},{12,16},{16,20},{20,24},{24,28},{1,5},{5,9},{9,... | collective-permute-start | bytes 393224 | tf_op jit(solution)/shard_map/while/body/eval_jaxpr/ppermute | solution.py:16
  26.0 4.3 %collective-permute-start.1 = (bf16[256,2,128]{2,0,1:T(8,128)(2,1)}, bf16[256,2,128]{2,0,1:T(8,128)(2,1)S(1)}, u32[]{:S(2)}, u32[]{:S(2)}) collective-permute-start(bf16[256,2,128]{2,0,1:T(8,128)(2,1)} %get-tuple-element.301), channel_id=1, source_target_pairs={{0,4},{4,8},{8,12},{12,16},{16,20},{20,24},{24,28},{1,5},{5,9},{9,... | collective-permute-start | bytes 393224 | tf_op jit(solution)/shard_map/while/body/eval_jaxpr/ppermute | solution.py:16
  35.1 4.2 %collective-permute-start = (bf16[256,2,128]{2,0,1:T(8,128)(2,1)S(1)}, bf16[256,2,128]{2,0,1:T(8,128)(2,1)S(1)}, u32[]{:S(2)}, u32[]{:S(2)}) collective-permute-start(bf16[256,2,128]{2,0,1:T(8,128)(2,1)S(1)} %get-tuple-element.300), channel_id=1, source_target_pairs={{0,4},{4,8},{8,12},{12,16},{16,20},{20,24},{24,28},{1,5},{5,9},{9,... | collective-permute-start | bytes 393224 | tf_op jit(solution)/shard_map/while/body/eval_jaxpr/ppermute | solution.py:16
  39.3 3.5 %collective-permute-start.1 = (bf16[256,2,128]{2,0,1:T(8,128)(2,1)}, bf16[256,2,128]{2,0,1:T(8,128)(2,1)S(1)}, u32[]{:S(2)}, u32[]{:S(2)}) collective-permute-start(bf16[256,2,128]{2,0,1:T(8,128)(2,1)} %get-tuple-element.301), channel_id=1, source_target_pairs={{0,4},{4,8},{8,12},{12,16},{16,20},{20,24},{24,28},{1,5},{5,9},{9,... | collective-permute-start | bytes 393224 | tf_op jit(solution)/shard_map/while/body/eval_jaxpr/ppermute | solution.py:16
  43.0 1.4 %fusion.40 = (f32[2,2,256]{2,1,0:T(2,128)S(1)}, bf16[2,2,256,256]{2,3,1,0:T(8,128)(2,1)S(1)}) fusion(bf16[256,2,2,128]{3,0,2,1:T(8,128)(2,1)} %get-tuple-element.315, bf16[256,2,128]{2,0,1:T(8,128)(2,1)S(1)} %collective-permute-done, pred[256,256]{0,1:T(8,128)(4,1)S(1)} %fusion.39), kind=kOutput, calls=%fused_computation.53.clone.1 | convolution fusion | flops 68418560 | bytes 987136 | tf_op jit(solution)/shard_map/while/body/eval_jaxpr/sgrh,kgh->grsk/dot_general | solution.py:41
  47.5 4.2 %collective-permute-start = (bf16[256,2,128]{2,0,1:T(8,128)(2,1)S(1)}, bf16[256,2,128]{2,0,1:T(8,128)(2,1)S(1)}, u32[]{:S(2)}, u32[]{:S(2)}) collective-permute-start(bf16[256,2,128]{2,0,1:T(8,128)(2,1)S(1)} %get-tuple-element.300), channel_id=1, source_target_pairs={{0,4},{4,8},{8,12},{12,16},{16,20},{20,24},{24,28},{1,5},{5,9},{9,... | collective-permute-start | bytes 393224 | tf_op jit(solution)/shard_map/while/body/eval_jaxpr/ppermute | solution.py:16
  51.7 4.3 %collective-permute-start.1 = (bf16[256,2,128]{2,0,1:T(8,128)(2,1)}, bf16[256,2,128]{2,0,1:T(8,128)(2,1)S(1)}, u32[]{:S(2)}, u32[]{:S(2)}) collective-permute-start(bf16[256,2,128]{2,0,1:T(8,128)(2,1)} %get-tuple-element.301), channel_id=1, source_target_pairs={{0,4},{4,8},{8,12},{12,16},{16,20},{20,24},{24,28},{1,5},{5,9},{9,... | collective-permute-start | bytes 393224 | tf_op jit(solution)/shard_map/while/body/eval_jaxpr/ppermute | solution.py:16
  60.7 4.2 %collective-permute-start = (bf16[256,2,128]{2,0,1:T(8,128)(2,1)S(1)}, bf16[256,2,128]{2,0,1:T(8,128)(2,1)S(1)}, u32[]{:S(2)}, u32[]{:S(2)}) collective-permute-start(bf16[256,2,128]{2,0,1:T(8,128)(2,1)S(1)} %get-tuple-element.300), channel_id=1, source_target_pairs={{0,4},{4,8},{8,12},{12,16},{16,20},{20,24},{24,28},{1,5},{5,9},{9,... | collective-permute-start | bytes 393224 | tf_op jit(solution)/shard_map/while/body/eval_jaxpr/ppermute | solution.py:16
  65.0 3.5 %collective-permute-start.1 = (bf16[256,2,128]{2,0,1:T(8,128)(2,1)}, bf16[256,2,128]{2,0,1:T(8,128)(2,1)S(1)}, u32[]{:S(2)}, u32[]{:S(2)}) collective-permute-start(bf16[256,2,128]{2,0,1:T(8,128)(2,1)} %get-tuple-element.301), channel_id=1, source_target_pairs={{0,4},{4,8},{8,12},{12,16},{16,20},{20,24},{24,28},{1,5},{5,9},{9,... | collective-permute-start | bytes 393224 | tf_op jit(solution)/shard_map/while/body/eval_jaxpr/ppermute | solution.py:16
  73.1 4.2 %collective-permute-start = (bf16[256,2,128]{2,0,1:T(8,128)(2,1)S(1)}, bf16[256,2,128]{2,0,1:T(8,128)(2,1)S(1)}, u32[]{:S(2)}, u32[]{:S(2)}) collective-permute-start(bf16[256,2,128]{2,0,1:T(8,128)(2,1)S(1)} %get-tuple-element.300), channel_id=1, source_target_pairs={{0,4},{4,8},{8,12},{12,16},{16,20},{20,24},{24,28},{1,5},{5,9},{9,... | collective-permute-start | bytes 393224 | tf_op jit(solution)/shard_map/while/body/eval_jaxpr/ppermute | solution.py:16
  77.4 4.3 %collective-permute-start.1 = (bf16[256,2,128]{2,0,1:T(8,128)(2,1)}, bf16[256,2,128]{2,0,1:T(8,128)(2,1)S(1)}, u32[]{:S(2)}, u32[]{:S(2)}) collective-permute-start(bf16[256,2,128]{2,0,1:T(8,128)(2,1)} %get-tuple-element.301), channel_id=1, source_target_pairs={{0,4},{4,8},{8,12},{12,16},{16,20},{20,24},{24,28},{1,5},{5,9},{9,... | collective-permute-start | bytes 393224 | tf_op jit(solution)/shard_map/while/body/eval_jaxpr/ppermute | solution.py:16
  86.4 4.2 %collective-permute-start = (bf16[256,2,128]{2,0,1:T(8,128)(2,1)S(1)}, bf16[256,2,128]{2,0,1:T(8,128)(2,1)S(1)}, u32[]{:S(2)}, u32[]{:S(2)}) collective-permute-start(bf16[256,2,128]{2,0,1:T(8,128)(2,1)S(1)} %get-tuple-element.300), channel_id=1, source_target_pairs={{0,4},{4,8},{8,12},{12,16},{16,20},{20,24},{24,28},{1,5},{5,9},{9,... | collective-permute-start | bytes 393224 | tf_op jit(solution)/shard_map/while/body/eval_jaxpr/ppermute | solution.py:16
  90.6 3.5 %collective-permute-start.1 = (bf16[256,2,128]{2,0,1:T(8,128)(2,1)}, bf16[256,2,128]{2,0,1:T(8,128)(2,1)S(1)}, u32[]{:S(2)}, u32[]{:S(2)}) collective-permute-start(bf16[256,2,128]{2,0,1:T(8,128)(2,1)} %get-tuple-element.301), channel_id=1, source_target_pairs={{0,4},{4,8},{8,12},{12,16},{16,20},{20,24},{24,28},{1,5},{5,9},{9,... | collective-permute-start | bytes 393224 | tf_op jit(solution)/shard_map/while/body/eval_jaxpr/ppermute | solution.py:16
  100.1 1.7 %collective-permute-start.3 = (bf16[256,4,128]{2,0,1:T(8,128)(2,1)S(1)}, bf16[256,4,128]{2,0,1:T(8,128)(2,1)}, u32[]{:S(2)}, u32[]{:S(2)}) collective-permute-start(bf16[256,4,128]{2,0,1:T(8,128)(2,1)S(1)} %bitcast.50), channel_id=1, source_target_pairs={{0,3},{1,0},{2,1},{3,2},{4,7},{5,4},{6,5},{7,6},{8,11},{9,8},{10,9... | collective-permute-start | bytes 786440 | tf_op jit(solution)/shard_map/ppermute | solution.py:113
  101.9 5.1 %collective-permute-done.2 = bf16[256,4,128]{2,0,1:T(8,128)(2,1)} collective-permute-done((bf16[256,4,128]{2,0,1:T(8,128)(2,1)S(1)}, bf16[256,4,128]{2,0,1:T(8,128)(2,1)}, u32[]{:S(2)}, u32[]{:S(2)}) %collective-permute-start.2) | collective-permute-done | bytes 262176 | tf_op jit(solution)/shard_map/ppermute | solution.py:108
  109.7 1.7 %constant_dynamic-update-slice_fusion.2 = bf16[256,16,128]{2,0,1:T(8,128)(2,1)} fusion(bf16[256,16,128]{2,0,1:T(8,128)(2,1)} %constant_dynamic-update-slice_fusion.3, bf16[256,4,128]{2,0,1:T(8,128)(2,1)} %collective-permute-done.2, s32[]{:T(128)S(6)} %select_n.44), kind=kLoop, calls=%fused_computation.48 | loop fusion | bytes 524292 | tf_op jit(solution)/shard_map/dynamic_update_slice | solution.py:109
  111.3 1.7 %constant_dynamic-update-slice_fusion.1 = bf16[256,16,128]{2,0,1:T(8,128)(2,1)} fusion(bf16[256,16,128]{2,0,1:T(8,128)(2,1)} %constant_dynamic-update-slice_fusion.2, bf16[256,4,128]{2,0,1:T(8,128)(2,1)} %collective-permute-done.3, s32[]{:T(128)S(6)} %select_n.46), kind=kLoop, calls=%fused_computation.47 | loop fusion | bytes 524292 | tf_op jit(solution)/shard_map/dynamic_update_slice | solution.py:114
  113.1 1.7 %constant_dynamic-update-slice_fusion = bf16[256,16,128]{2,0,1:T(8,128)(2,1)} fusion(bf16[256,16,128]{2,0,1:T(8,128)(2,1)} %constant_dynamic-update-slice_fusion.1, bf16[256,4,128]{2,0,1:T(8,128)(2,1)} %collective-permute-done.4, s32[]{:T(128)S(6)} %select_n.48), kind=kLoop, calls=%fused_computation.46 | loop fusion | bytes 524292 | tf_op jit(solution)/shard_map/dynamic_update_slice | solution.py:109
  114.8 3.1 %multiply_reduce_fusion = (f32[256]{0:T(256)S(1)}, f32[256,768]{1,0:T(8,128)}) fusion(bf16[256,16,128]{2,0,1:T(8,128)(2,1)} %constant_dynamic-update-slice_fusion, bf16[16,128,768]{2,1,0:T(8,128)(2,1)S(1)} %copy-done), kind=kOutput, calls=%fused_computation.25 | convolution fusion | flops 805699328 | bytes 4981760 | tf_op jit(solution)/shard_map/dot_general | solution.py:119
  117.9 8.2 %psum.7 = f32[256]{0:T(256)S(1)} all-reduce(f32[256]{0:T(256)S(1)} %get-tuple-element.225), channel_id=1, replica_groups=mesh['ctx'=8,'tp'=4] {'tp'}, use_global_device_ids=true, to_apply=%region_5.6 | all-reduce | flops 256 | bytes 2048 | tf_op jit(solution)/shard_map/psum | solution.py:122
  126.1 2.1 %add_convert_fusion = bf16[256,768]{1,0:T(8,128)(2,1)} fusion(f32[256,768]{1,0:T(8,128)} %get-tuple-element.226, bf16[256,768]{1,0:T(8,128)(2,1)S(1)} %copy-done.4, f32[768]{0:T(1024)S(1)} %convert_element_type.50, f32[256]{0:T(256)S(1)} %add_rsqrt_fusion), kind=kLoop, calls=%fused_computation.24 | loop fusion | flops 983040 | bytes 1576960 | tf_op jit(solution)/shard_map/convert_element_type | solution.py:125
  (139 shorter events, 43.6 us)
Async XLA Ops:
  0.0 114.8 %copy-start = (bf16[16,128,768]{2,1,0:T(8,128)(2,1)S(1)}, bf16[16,128,768]{2,1,0:T(8,128)(2,1)}, u32[]{:S(2)}) copy-start(bf16[16,128,768]{2,1,0:T(8,128)(2,1)} %param.12) | copy-start | bytes 9437188
  0.0 4.0 %copy-start.3 = (bf16[256,2,128]{2,1,0:T(2,128)(2,1)S(1)}, bf16[256,2,128]{2,1,0:T(2,128)(2,1)}, u32[]{:S(2)}) copy-start(bf16[256,2,128]{2,1,0:T(2,128)(2,1)} %param.10) | copy-start | bytes 393220
  8.8 8.5 %collective-permute-start = (bf16[256,2,128]{2,0,1:T(8,128)(2,1)S(1)}, bf16[256,2,128]{2,0,1:T(8,128)(2,1)S(1)}, u32[]{:S(2)}, u32[]{:S(2)}) collective-permute-start(bf16[256,2,128]{2,0,1:T(8,128)(2,1)S(1)} %get-tuple-element.300), channel_id=1, source_target_pairs={{0,4},{4,8},{8,12},{12,16},{16,20},{20,24},{24,28},{1,5},{5,9},{9,... | collective-permute-start | bytes 393224 | tf_op jit(solution)/shard_map/while/body/eval_jaxpr/ppermute | solution.py:16
  13.6 6.2 %collective-permute-start.1 = (bf16[256,2,128]{2,0,1:T(8,128)(2,1)}, bf16[256,2,128]{2,0,1:T(8,128)(2,1)S(1)}, u32[]{:S(2)}, u32[]{:S(2)}) collective-permute-start(bf16[256,2,128]{2,0,1:T(8,128)(2,1)} %get-tuple-element.301), channel_id=1, source_target_pairs={{0,4},{4,8},{8,12},{12,16},{16,20},{20,24},{24,28},{1,5},{5,9},{9,... | collective-permute-start | bytes 393224 | tf_op jit(solution)/shard_map/while/body/eval_jaxpr/ppermute | solution.py:16
  17.1 3.4 %copy-start.1 = (f32[2,2,256,128]{3,2,1,0:T(8,128)S(1)}, f32[2,2,256,128]{3,2,1,0:T(8,128)}, u32[]{:S(2)}) copy-start(f32[2,2,256,128]{3,2,1,0:T(8,128)} %get-tuple-element.298) | copy-start | bytes 1572868 | tf_op jit(solution)/shard_map/while
  21.8 8.8 %collective-permute-start = (bf16[256,2,128]{2,0,1:T(8,128)(2,1)S(1)}, bf16[256,2,128]{2,0,1:T(8,128)(2,1)S(1)}, u32[]{:S(2)}, u32[]{:S(2)}) collective-permute-start(bf16[256,2,128]{2,0,1:T(8,128)(2,1)S(1)} %get-tuple-element.300), channel_id=1, source_target_pairs={{0,4},{4,8},{8,12},{12,16},{16,20},{20,24},{24,28},{1,5},{5,9},{9,... | collective-permute-start | bytes 393224 | tf_op jit(solution)/shard_map/while/body/eval_jaxpr/ppermute | solution.py:16
  26.0 7.2 %collective-permute-start.1 = (bf16[256,2,128]{2,0,1:T(8,128)(2,1)}, bf16[256,2,128]{2,0,1:T(8,128)(2,1)S(1)}, u32[]{:S(2)}, u32[]{:S(2)}) collective-permute-start(bf16[256,2,128]{2,0,1:T(8,128)(2,1)} %get-tuple-element.301), channel_id=1, source_target_pairs={{0,4},{4,8},{8,12},{12,16},{16,20},{20,24},{24,28},{1,5},{5,9},{9,... | collective-permute-start | bytes 393224 | tf_op jit(solution)/shard_map/while/body/eval_jaxpr/ppermute | solution.py:16
  35.1 7.9 %collective-permute-start = (bf16[256,2,128]{2,0,1:T(8,128)(2,1)S(1)}, bf16[256,2,128]{2,0,1:T(8,128)(2,1)S(1)}, u32[]{:S(2)}, u32[]{:S(2)}) collective-permute-start(bf16[256,2,128]{2,0,1:T(8,128)(2,1)S(1)} %get-tuple-element.300), channel_id=1, source_target_pairs={{0,4},{4,8},{8,12},{12,16},{16,20},{20,24},{24,28},{1,5},{5,9},{9,... | collective-permute-start | bytes 393224 | tf_op jit(solution)/shard_map/while/body/eval_jaxpr/ppermute | solution.py:16
  39.3 6.3 %collective-permute-start.1 = (bf16[256,2,128]{2,0,1:T(8,128)(2,1)}, bf16[256,2,128]{2,0,1:T(8,128)(2,1)S(1)}, u32[]{:S(2)}, u32[]{:S(2)}) collective-permute-start(bf16[256,2,128]{2,0,1:T(8,128)(2,1)} %get-tuple-element.301), channel_id=1, source_target_pairs={{0,4},{4,8},{8,12},{12,16},{16,20},{20,24},{24,28},{1,5},{5,9},{9,... | collective-permute-start | bytes 393224 | tf_op jit(solution)/shard_map/while/body/eval_jaxpr/ppermute | solution.py:16
  42.8 3.4 %copy-start.1 = (f32[2,2,256,128]{3,2,1,0:T(8,128)S(1)}, f32[2,2,256,128]{3,2,1,0:T(8,128)}, u32[]{:S(2)}) copy-start(f32[2,2,256,128]{3,2,1,0:T(8,128)} %get-tuple-element.298) | copy-start | bytes 1572868 | tf_op jit(solution)/shard_map/while
  47.5 8.7 %collective-permute-start = (bf16[256,2,128]{2,0,1:T(8,128)(2,1)S(1)}, bf16[256,2,128]{2,0,1:T(8,128)(2,1)S(1)}, u32[]{:S(2)}, u32[]{:S(2)}) collective-permute-start(bf16[256,2,128]{2,0,1:T(8,128)(2,1)S(1)} %get-tuple-element.300), channel_id=1, source_target_pairs={{0,4},{4,8},{8,12},{12,16},{16,20},{20,24},{24,28},{1,5},{5,9},{9,... | collective-permute-start | bytes 393224 | tf_op jit(solution)/shard_map/while/body/eval_jaxpr/ppermute | solution.py:16
  51.7 7.1 %collective-permute-start.1 = (bf16[256,2,128]{2,0,1:T(8,128)(2,1)}, bf16[256,2,128]{2,0,1:T(8,128)(2,1)S(1)}, u32[]{:S(2)}, u32[]{:S(2)}) collective-permute-start(bf16[256,2,128]{2,0,1:T(8,128)(2,1)} %get-tuple-element.301), channel_id=1, source_target_pairs={{0,4},{4,8},{8,12},{12,16},{16,20},{20,24},{24,28},{1,5},{5,9},{9,... | collective-permute-start | bytes 393224 | tf_op jit(solution)/shard_map/while/body/eval_jaxpr/ppermute | solution.py:16
  56.1 3.4 %copy-start.1 = (f32[2,2,256,128]{3,2,1,0:T(8,128)S(1)}, f32[2,2,256,128]{3,2,1,0:T(8,128)}, u32[]{:S(2)}) copy-start(f32[2,2,256,128]{3,2,1,0:T(8,128)} %get-tuple-element.298) | copy-start | bytes 1572868 | tf_op jit(solution)/shard_map/while
  60.7 7.9 %collective-permute-start = (bf16[256,2,128]{2,0,1:T(8,128)(2,1)S(1)}, bf16[256,2,128]{2,0,1:T(8,128)(2,1)S(1)}, u32[]{:S(2)}, u32[]{:S(2)}) collective-permute-start(bf16[256,2,128]{2,0,1:T(8,128)(2,1)S(1)} %get-tuple-element.300), channel_id=1, source_target_pairs={{0,4},{4,8},{8,12},{12,16},{16,20},{20,24},{24,28},{1,5},{5,9},{9,... | collective-permute-start | bytes 393224 | tf_op jit(solution)/shard_map/while/body/eval_jaxpr/ppermute | solution.py:16
  65.0 6.3 %collective-permute-start.1 = (bf16[256,2,128]{2,0,1:T(8,128)(2,1)}, bf16[256,2,128]{2,0,1:T(8,128)(2,1)S(1)}, u32[]{:S(2)}, u32[]{:S(2)}) collective-permute-start(bf16[256,2,128]{2,0,1:T(8,128)(2,1)} %get-tuple-element.301), channel_id=1, source_target_pairs={{0,4},{4,8},{8,12},{12,16},{16,20},{20,24},{24,28},{1,5},{5,9},{9,... | collective-permute-start | bytes 393224 | tf_op jit(solution)/shard_map/while/body/eval_jaxpr/ppermute | solution.py:16
  73.1 8.7 %collective-permute-start = (bf16[256,2,128]{2,0,1:T(8,128)(2,1)S(1)}, bf16[256,2,128]{2,0,1:T(8,128)(2,1)S(1)}, u32[]{:S(2)}, u32[]{:S(2)}) collective-permute-start(bf16[256,2,128]{2,0,1:T(8,128)(2,1)S(1)} %get-tuple-element.300), channel_id=1, source_target_pairs={{0,4},{4,8},{8,12},{12,16},{16,20},{20,24},{24,28},{1,5},{5,9},{9,... | collective-permute-start | bytes 393224 | tf_op jit(solution)/shard_map/while/body/eval_jaxpr/ppermute | solution.py:16
  77.4 7.1 %collective-permute-start.1 = (bf16[256,2,128]{2,0,1:T(8,128)(2,1)}, bf16[256,2,128]{2,0,1:T(8,128)(2,1)S(1)}, u32[]{:S(2)}, u32[]{:S(2)}) collective-permute-start(bf16[256,2,128]{2,0,1:T(8,128)(2,1)} %get-tuple-element.301), channel_id=1, source_target_pairs={{0,4},{4,8},{8,12},{12,16},{16,20},{20,24},{24,28},{1,5},{5,9},{9,... | collective-permute-start | bytes 393224 | tf_op jit(solution)/shard_map/while/body/eval_jaxpr/ppermute | solution.py:16
  86.4 7.9 %collective-permute-start = (bf16[256,2,128]{2,0,1:T(8,128)(2,1)S(1)}, bf16[256,2,128]{2,0,1:T(8,128)(2,1)S(1)}, u32[]{:S(2)}, u32[]{:S(2)}) collective-permute-start(bf16[256,2,128]{2,0,1:T(8,128)(2,1)S(1)} %get-tuple-element.300), channel_id=1, source_target_pairs={{0,4},{4,8},{8,12},{12,16},{16,20},{20,24},{24,28},{1,5},{5,9},{9,... | collective-permute-start | bytes 393224 | tf_op jit(solution)/shard_map/while/body/eval_jaxpr/ppermute | solution.py:16
  90.6 6.3 %collective-permute-start.1 = (bf16[256,2,128]{2,0,1:T(8,128)(2,1)}, bf16[256,2,128]{2,0,1:T(8,128)(2,1)S(1)}, u32[]{:S(2)}, u32[]{:S(2)}) collective-permute-start(bf16[256,2,128]{2,0,1:T(8,128)(2,1)} %get-tuple-element.301), channel_id=1, source_target_pairs={{0,4},{4,8},{8,12},{12,16},{16,20},{20,24},{24,28},{1,5},{5,9},{9,... | collective-permute-start | bytes 393224 | tf_op jit(solution)/shard_map/while/body/eval_jaxpr/ppermute | solution.py:16
  94.1 3.4 %copy-start.1 = (f32[2,2,256,128]{3,2,1,0:T(8,128)S(1)}, f32[2,2,256,128]{3,2,1,0:T(8,128)}, u32[]{:S(2)}) copy-start(f32[2,2,256,128]{3,2,1,0:T(8,128)} %get-tuple-element.298) | copy-start | bytes 1572868 | tf_op jit(solution)/shard_map/while
  100.1 6.9 %collective-permute-start.2 = (bf16[256,4,128]{2,0,1:T(8,128)(2,1)S(1)}, bf16[256,4,128]{2,0,1:T(8,128)(2,1)}, u32[]{:S(2)}, u32[]{:S(2)}) collective-permute-start(bf16[256,4,128]{2,0,1:T(8,128)(2,1)S(1)} %bitcast.49), channel_id=1, source_target_pairs={{0,1},{1,2},{2,3},{3,0},{4,5},{5,6},{6,7},{7,4},{8,9},{9,10},{10,1... | collective-permute-start | bytes 786440 | tf_op jit(solution)/shard_map/ppermute | solution.py:108
  100.1 11.2 %collective-permute-start.3 = (bf16[256,4,128]{2,0,1:T(8,128)(2,1)S(1)}, bf16[256,4,128]{2,0,1:T(8,128)(2,1)}, u32[]{:S(2)}, u32[]{:S(2)}) collective-permute-start(bf16[256,4,128]{2,0,1:T(8,128)(2,1)S(1)} %bitcast.50), channel_id=1, source_target_pairs={{0,3},{1,0},{2,1},{3,2},{4,7},{5,4},{6,5},{7,6},{8,11},{9,8},{10,9... | collective-permute-start | bytes 786440 | tf_op jit(solution)/shard_map/ppermute | solution.py:113
  106.9 6.1 %collective-permute-start.4 = (bf16[256,4,128]{2,0,1:T(8,128)(2,1)}, bf16[256,4,128]{2,0,1:T(8,128)(2,1)}, u32[]{:S(2)}, u32[]{:S(2)}) collective-permute-start(bf16[256,4,128]{2,0,1:T(8,128)(2,1)} %collective-permute-done.2), channel_id=1, source_target_pairs={{0,1},{1,2},{2,3},{3,0},{4,5},{5,6},{6,7},{7,4},{8,9},{9,10},{10,1... | collective-permute-start | bytes 786440 | tf_op jit(solution)/shard_map/ppermute | solution.py:108
  113.0 13.1 %copy-start.4 = (bf16[256,768]{1,0:T(8,128)(2,1)S(1)}, bf16[256,768]{1,0:T(8,128)(2,1)}, u32[]{:S(2)}) copy-start(bf16[256,768]{1,0:T(8,128)(2,1)} %param.11) | copy-start | bytes 1179652
  (12 other events, 22.0 us)
